TPU v7x, 32 devices: a whole 2x2x4 slice. The times are simulated.
32 devices in a mesh: rows: 8 (over z, y), sub: 4 (over x, core).
Axes of the slice: x: 2, y: 2, z: 4, core: 2. Of those that a mesh axis runs over, the one named last changes fastest.
Arguments:
- held: float32 [512, 4, 128, 256], P('rows', 'sub'), may hold values from -256 to 256
- held_block: int32 [512, 4], P('rows', 'sub'), may hold values from 0 to 255, as said below
- held_count: int32 [8, 4], P('rows', 'sub'), may hold values from 0 to 64
Outputs:
- q_factor: float32 [256, 4, 128, 256], P('rows', 'sub')
- r_factor: float32 [256, 256], replicated
Inputs may be any that keep to these rules, and one draw needn't show every extreme that they name: `held_block`: for slots j < held_count of a device, the ids are block numbers of its column group; over all devices of a column group each block is held in exactly one such slot. Slots at or past held_count hold arbitrary ids and data. A device holds at most 8 blocks whose number b has b // 32 equal to any one given device index along rows, and some device reaches that.
All inputs are finite; a program needn't handle non-finite values.
Results may differ from a plain program's by a relative error of at most 0.0003.
Values sent between devices are 32-bit elements; how exact they have to be, the bound alone decides.
No kernel may reach another device: no remote copies, remote signals or barrier semaphores. Data moves between devices by JAX's collectives and lax.ppermute only.
A program may use at most 128 MiB of HBM per device.

v0:
```python
import jax
import jax.numpy as jnp
from jax import lax
from jax.sharding import PartitionSpec as P

BLK_DEV = 32


def factor(gram):
    lower = jnp.linalg.cholesky(gram)
    identity = jnp.eye(gram.shape[0], dtype=gram.dtype)
    inverse = lax.linalg.triangular_solve(lower, identity, left_side=True, lower=True)
    return (lower, inverse)


def gram_of(flattened, total):
    return (
        lax.dot_general(
            flattened,
            flattened,
            (((0,), (0,)), ((), ())),
            precision=lax.Precision.HIGHEST,
            preferred_element_type=jnp.float32,
        )
        / total
    )


def apply_inverse(flattened, inverse):
    return jnp.dot(
        flattened, inverse.T, precision=lax.Precision.HIGHEST, preferred_element_type=jnp.float32
    )


def reduce_gram(partial_value):
    return lax.psum(partial_value, ("rows", "sub"))


def per_device(held, held_block, held_count):
    capacity = held.shape[0]
    block_rows = held.shape[2]
    width = held.shape[3]
    devices_rows = lax.axis_size("rows")
    own_index = lax.axis_index("rows")
    per_slot = max(1, capacity // devices_rows)
    total = float(devices_rows * lax.axis_size("sub") * BLK_DEV * block_rows)
    blocks = held[:, 0]
    block_ids = held_block[:, 0]
    count = held_count[0, 0]
    slots = jnp.arange(capacity, dtype=jnp.int32)
    valid = slots < count
    destination = block_ids // BLK_DEV
    earlier = (
        (destination[:, None] == destination[None, :])
        & valid[None, :]
        & (slots[None, :] < slots[:, None])
    )
    rank_within = jnp.sum(earlier.astype(jnp.int32), axis=1)
    target = jnp.where(valid, destination * per_slot + rank_within, devices_rows * per_slot)
    labels_out = block_ids.astype(jnp.float32)
    outgoing = (
        jnp.zeros((devices_rows * per_slot, block_rows, width), jnp.float32)
        .at[target]
        .set(blocks, mode="drop")
    )
    labels = (
        jnp.full((devices_rows * per_slot,), -1.0, jnp.float32)
        .at[target]
        .set(labels_out, mode="drop")
    )
    arrived = lax.all_to_all(outgoing, "rows", split_axis=0, concat_axis=0, tiled=True)
    arrived_labels = lax.all_to_all(labels, "rows", split_axis=0, concat_axis=0, tiled=True)
    local = arrived_labels.astype(jnp.int32) - own_index * BLK_DEV
    place = jnp.where(arrived_labels >= 0.0, local, BLK_DEV)
    resident = (
        jnp.zeros((BLK_DEV, block_rows, width), jnp.float32).at[place].set(arrived, mode="drop")
    )
    flattened = resident.reshape(-1, width)
    partial_one = gram_of(flattened, total)
    lower_one, inverse_one = factor(reduce_gram(partial_one))
    first = apply_inverse(flattened, inverse_one)
    lower_two, inverse_two = factor(reduce_gram(gram_of(first, total)))
    second, lower_one, lower_two = (apply_inverse(first, inverse_two), lower_one, lower_two)
    result = second.reshape(BLK_DEV, block_rows, width)
    r_factor = jnp.dot(
        lower_two.T,
        lower_one.T,
        precision=lax.Precision.HIGHEST,
        preferred_element_type=jnp.float32,
    )
    return (result[:, None], r_factor)


def solution(mesh):
    in_specs = (P("rows", "sub", None, None), P("rows", "sub"), P("rows", "sub"))
    out_specs = (P("rows", "sub", None, None), P())
    return jax.shard_map(
        per_device, mesh=mesh, in_specs=in_specs, out_specs=out_specs, check_vma=False
    )
```

profile of v0, /device:TPU:0, one launch (start us, length us, event | category | flops | bytes accessed | tf_op | source)
XLA Modules:
  0.0 661.5 jit_solution(13611043332102278474)
XLA Ops:
  7.2 0.7 bitcast_convert_fusion
  7.8 0.7 and_select_fusion
  9.3 0.8 scatter_custom_fusion
  10.1 0.7 all_to_all.9
  10.8 7.3 %all-to-all-start = ((f32[8,8,1]{1,2,0:T(1,128)}), f32[8,8,1]{1,2,0:T(1,128)S(1)}, u32[]{:S(2)}, u32[]{:S(2)}) async-start(f32[8,8,1]{1,2,0:T(1,128)} %bitcast.5), calls=%async_computation | async-start | bytes 8192 | tf_op jit(solution)/shard_map/all_to_all | solution.py:72
  18.1 4.2 broadcast_in_dim.26
  22.3 16.0 %scatter_fusion = f32[64,128,256]{2,1,0:T(8,128)} fusion(f32[64,128,256]{2,1,0:T(8,128)} %broadcast_in_dim.26, s32[64]{0:T(128)S(1)} %fusion.38, f32[64,128,256]{2,1,0:T(8,128)} %bitcast.102), kind=kCustom, calls=%fused_computation.1 | custom fusion | bytes 25166080 | tf_op jit(solution)/shard_map/scatter | solution.py:64
  38.4 5.8 all-to-all-start.1
  44.4 182.5 %all-to-all-done.1 = f32[64,128,256]{2,1,0:T(8,128)} async-done(((f32[64,128,256]{2,1,0:T(8,128)}), f32[64,128,256]{2,1,0:T(8,128)}, u32[]{:S(2)}, u32[]{:S(2)}) %all-to-all-start.1) | async-done | bytes 8388640 | tf_op jit(solution)/shard_map/all_to_all | solution.py:71
  226.9 2.5 broadcast_in_dim.11
  229.4 15.4 %scatter_fusion.1 = f32[32,128,256]{2,1,0:T(8,128)} fusion(f32[32,128,256]{2,1,0:T(8,128)} %broadcast_in_dim.11, s32[64]{0:T(128)S(1)} %fusion.37, f32[64,128,256]{2,1,0:T(8,128)} %all-to-all-done.1), kind=kCustom, calls=%fused_computation.2 | custom fusion | bytes 25166080 | tf_op jit(solution)/shard_map/scatter | solution.py:76
  244.8 10.9 %fusion = f32[256,256]{0,1:T(8,128)} fusion(f32[32,128,256]{2,1,0:T(8,128)} %scatter_fusion.1), kind=kOutput, calls=%fused_computation.9 | convolution fusion | flops 3221291008 | bytes 4456448 | tf_op jit(solution)/shard_map/dot_general | solution.py:18
  256.0 124.2 %all-reduce.4.cloned.1.call-done = f32[256,256]{0,1:T(8,128)} async-done(((f32[256,256]{0,1:T(8,128)}), f32[256,256]{0,1:T(8,128)}) %all-reduce.4.cloned.1.call-update) | async-done | bytes 262160 | tf_op jit(solution)/shard_map/psum | solution.py:36
  380.2 1.1 copy.27
  381.3 1.0 fusion.10
  382.3 11.7 %cholesky.130 = f32[128,128]{1,0:T(8,128)S(1)} custom-call(f32[128,128]{1,0:T(8,128)S(1)} %cholesky.194), custom_call_target="Cholesky" | custom-call | tf_op jit(solution)/shard_map/jit(cholesky)/cholesky | solution.py:10
  394.0 9.8 %custom-call.13 = f32[1,128,128]{1,2,0:T(8,128)S(1)} custom-call(f32[1,128,128]{2,1,0:T(8,128)S(1)} %get-tuple-element.55), custom_call_target="InvertDiagBlocksLowerTriangular" | custom-call | tf_op jit(solution)/shard_map/jit(cholesky)/cholesky | solution.py:10
  404.4 11.7 %cholesky.147 = f32[128,128]{1,0:T(8,128)S(1)} custom-call(f32[128,128]{1,0:T(8,128)S(1)} %convolution_subtract_fusion.3), custom_call_target="Cholesky" | custom-call | tf_op jit(solution)/shard_map/jit(cholesky)/cholesky | solution.py:10
  416.1 0.7 compare_reduce_fusion.2
  418.3 4.1 while.4
  418.3 0.6 fusion.63
  418.9 1.4 bitcast_dynamic-update-slice_fusion.4
  420.4 0.6 fusion.63
  421.0 1.4 bitcast_dynamic-update-slice_fusion.4
  422.4 19.7 %custom-call.14 = f32[2,128,128]{1,2,0:T(8,128)S(1)} custom-call(f32[2,128,128]{2,1,0:T(8,128)S(1)} %get-tuple-element.18), custom_call_target="InvertDiagBlocksLowerTriangular" | custom-call | tf_op jit(solution)/shard_map/triangular_solve/custom-call.0 | solution.py:12
  442.1 0.3 fusion.23
  442.7 0.3 fusion.30
  443.0 5.5 fusion.1
  448.5 1.9 copy-done
  450.4 7.4 %convolution_multiply_fusion = f32[256,256]{0,1:T(8,128)} fusion(f32[4096,256]{1,0:T(8,128)S(1)} %fusion.1), kind=kOutput, calls=%fused_computation.7 | convolution fusion | flops 3221291008 | bytes 4456448 | tf_op jit(solution)/shard_map/dot_general | solution.py:18
  457.9 124.1 %all-reduce.6.cloned.1.call-done = f32[256,256]{0,1:T(8,128)} async-done(((f32[256,256]{0,1:T(8,128)}), f32[256,256]{0,1:T(8,128)}) %all-reduce.6.cloned.1.call-update) | async-done | bytes 262160 | tf_op jit(solution)/shard_map/psum | solution.py:36
  582.0 1.1 copy.29
  583.1 1.0 fusion.9
  584.1 11.7 %cholesky.164 = f32[128,128]{1,0:T(8,128)S(1)} custom-call(f32[128,128]{1,0:T(8,128)S(1)} %cholesky.197), custom_call_target="Cholesky" | custom-call | tf_op jit(solution)/shard_map/jit(cholesky)/cholesky | solution.py:10
  595.9 10.2 %custom-call.15 = f32[1,128,128]{1,2,0:T(8,128)S(1)} custom-call(f32[1,128,128]{2,1,0:T(8,128)S(1)} %get-tuple-element.51), custom_call_target="InvertDiagBlocksLowerTriangular" | custom-call | tf_op jit(solution)/shard_map/jit(cholesky)/cholesky | solution.py:10
  606.6 11.7 %cholesky.181 = f32[128,128]{1,0:T(8,128)S(1)} custom-call(f32[128,128]{1,0:T(8,128)S(1)} %convolution_subtract_fusion.2), custom_call_target="Cholesky" | custom-call | tf_op jit(solution)/shard_map/jit(cholesky)/cholesky | solution.py:10
  618.3 0.6 compare_reduce_fusion
  619.0 0.6 compare_reduce_fusion.1
  620.9 1.2 fusion.15
  622.1 3.9 while.5
  622.2 0.6 fusion.64
  622.7 1.4 bitcast_dynamic-update-slice_fusion.5
  624.1 0.6 fusion.64
  624.7 1.4 bitcast_dynamic-update-slice_fusion.5
  626.1 19.8 %custom-call.16 = f32[2,128,128]{1,2,0:T(8,128)S(1)} custom-call(f32[2,128,128]{2,1,0:T(8,128)S(1)} %get-tuple-element.19), custom_call_target="InvertDiagBlocksLowerTriangular" | custom-call | tf_op jit(solution)/shard_map/triangular_solve/custom-call.0 | solution.py:12
  645.9 0.3 fusion.21
  646.5 0.3 fusion.26
  646.8 7.7 %fusion.5 = f32[4096,256]{1,0:T(8,128)} fusion(f32[4096,256]{1,0:T(8,128)} %copy-done, f32[128,256]{1,0:T(8,128)S(1)} %fusion.26, f32[128,256]{1,0:T(8,128)S(1)} %fusion.21), kind=kOutput, calls=%fused_computation.18 | convolution fusion | flops 3221291008 | bytes 8650752 | tf_op jit(solution)/shard_map/dot_general | solution.py:30
  (37 shorter events, 2.5 us)
Async XLA Ops:
  10.8 27.6 %all-to-all-start = ((f32[8,8,1]{1,2,0:T(1,128)}), f32[8,8,1]{1,2,0:T(1,128)S(1)}, u32[]{:S(2)}, u32[]{:S(2)}) async-start(f32[8,8,1]{1,2,0:T(1,128)} %bitcast.5), calls=%async_computation | async-start | bytes 8192 | tf_op jit(solution)/shard_map/all_to_all | solution.py:72
  38.4 188.5 %all-to-all-start.1 = ((f32[64,128,256]{2,1,0:T(8,128)}), f32[64,128,256]{2,1,0:T(8,128)}, u32[]{:S(2)}, u32[]{:S(2)}) async-start(f32[64,128,256]{2,1,0:T(8,128)} %scatter_fusion), calls=%async_computation.1 | async-start | bytes 16777216 | tf_op jit(solution)/shard_map/all_to_all | solution.py:71
  44.2 335.9 %all-reduce.4.cloned.1.call-start = ((), (), s32[]{:S(2)}) async-start(), calls=%async_computation.2 | async-start | bytes 524288 | tf_op jit(solution)/shard_map/psum | solution.py:36
  255.7 326.3 %all-reduce.6.cloned.1.call-start = ((), (), s32[]{:S(2)}) async-start(), calls=%async_computation.3 | async-start | bytes 524288 | tf_op jit(solution)/shard_map/psum | solution.py:36
  448.5 1.9 copy-start
Sparse Core Ops, SparseCore 0:
  255.8 124.3 all-reduce.3
  458.0 123.9 all-reduce.5
where the time goes:
time: 669 us; the launch traced here: 662 us
  waiting for transfers between devices  431 us (64%)
  other arithmetic  112 us (17%)
  local copies, waits for them, and re-layouts  51.9 us (8%)
  matrix products  35.4 us (5%)
  between operations  17.8 us (3%)
  starting transfers between devices  13.4 us (2%)
    psum x2, waiting for transfers between devices, reduce_gram(): return lax.psum(partial_value, ('rows', 'sub'))  248 us
    all_to_all x1, waiting for transfers between devices, per_device(): lax.all_to_all(outgoing, 'rows', split_axis=0, concat_axis=0, tiled=True)  182 us
    another operation x13, other arithmetic, factor(): lower = jnp.linalg.cholesky(gram)  69 us
    another operation x5, other arithmetic, factor(): lax.linalg.triangular_solve(lower, identity, left_side=True, lower=True)  39.6 us
    dot_general x2, matrix products, gram_of(): lax.dot_general(flattened, flattened, (((0,), (0,)), ((), ())), precision...  18.3 us
    scatter x1, local copies, waits for them, and re-layouts, per_device(): outgoing = jnp.zeros((devices_rows * per_slot, block_rows, width), jnp.fl...  16 us
    scatter x1, local copies, waits for them, and re-layouts, per_device(): jnp.zeros((BLK_DEV, block_rows, width), jnp.float32).at[place]  15.4 us
  transfers between devices with their start and end apart: 4, of which 3 were waited for; matrix products, arithmetic and copies ran while one was open for 3% of the time, Pallas kernels for 0%

commit v1 on v0

--- a/solution.py
+++ b/solution.py
@@ -33,7 +33,7 @@
 
 
 def reduce_gram(partial_value):
-    return lax.psum(partial_value, ("rows", "sub"))
+    return jnp.sum(lax.all_gather(partial_value, ("rows", "sub")), axis=0)
 
 
 def per_device(held, held_block, held_count):

time: 669 us -> 577 us (0.86)
  waiting for transfers between devices: 431 us -> 335 us
    psum x2 -> x0, waiting for transfers between devices: 248 us -> none  [reduce_gram(): return lax.psum(partial_value, ('rows', 'sub'))]
    all_gather x0 -> x2, waiting for transfers between devices: none -> 153 us  [reduce_gram(): return jnp.sum(lax.all_gather(partial_value, ('rows', 'sub')), axis=0)]
    reduce_sum x0 -> x2, other arithmetic: none -> 7.86 us  [reduce_gram(): return jnp.sum(lax.all_gather(partial_value, ('rows', 'sub')), axis=0)]
  transfers between devices with their start and end apart: 4 -> 4, of which waited for: 3 -> 3; matrix products, arithmetic and copies ran while one was open for 3% -> 4% of each run, Pallas kernels for 0% -> 0%
where the time goes in v1:
time: 577 us; the launch traced here: 570 us
  waiting for transfers between devices  335 us (58%)
  other arithmetic  118 us (20%)
  local copies, waits for them, and re-layouts  50.1 us (9%)
  matrix products  35.5 us (6%)
  between operations  17.7 us (3%)
  starting transfers between devices  13.4 us (2%)
    all_to_all x1, waiting for transfers between devices, per_device(): lax.all_to_all(outgoing, 'rows', split_axis=0, concat_axis=0, tiled=True)  182 us
    all_gather x2, waiting for transfers between devices, reduce_gram(): return jnp.sum(lax.all_gather(partial_value, ('rows', 'sub')), axis=0)  153 us
    another operation x13, other arithmetic, factor(): lower = jnp.linalg.cholesky(gram)  68.9 us
    another operation x5, other arithmetic, factor(): lax.linalg.triangular_solve(lower, identity, left_side=True, lower=True)  39.6 us
    dot_general x2, matrix products, gram_of(): lax.dot_general(flattened, flattened, (((0,), (0,)), ((), ())), precision...  18.4 us
    scatter x1, local copies, waits for them, and re-layouts, per_device(): outgoing = jnp.zeros((devices_rows * per_slot, block_rows, width), jnp.fl...  16 us
    scatter x1, local copies, waits for them, and re-layouts, per_device(): jnp.zeros((BLK_DEV, block_rows, width), jnp.float32).at[place]  15.4 us
    dot_general x2, matrix products, apply_inverse(): jnp.dot(flattened, inverse.T, precision=lax.Precision.HIGHEST, preferred_...  13.2 us
  transfers between devices with their start and end apart: 4, of which 3 were waited for; matrix products, arithmetic and copies ran while one was open for 4% of the time, Pallas kernels for 0%

profile of v1, /device:TPU:0, one launch (start us, length us, event | category | flops | bytes accessed | tf_op | source)
XLA Modules:
  0.0 570.0 jit_solution(9913125497328563449)
XLA Ops:
  7.2 0.7 bitcast_convert_fusion
  7.8 0.7 and_select_fusion
  9.3 0.8 scatter_custom_fusion
  10.1 0.7 all_to_all.9
  10.8 7.3 %all-to-all-start = ((f32[8,8,1]{1,2,0:T(1,128)}), f32[8,8,1]{1,2,0:T(1,128)S(1)}, u32[]{:S(2)}, u32[]{:S(2)}) async-start(f32[8,8,1]{1,2,0:T(1,128)} %bitcast.5), calls=%async_computation | async-start | bytes 8192 | tf_op jit(solution)/shard_map/all_to_all | solution.py:72
  18.1 4.2 broadcast_in_dim.26
  22.3 16.0 %scatter_fusion = f32[64,128,256]{2,1,0:T(8,128)} fusion(f32[64,128,256]{2,1,0:T(8,128)} %broadcast_in_dim.26, s32[64]{0:T(128)S(1)} %fusion.38, f32[64,128,256]{2,1,0:T(8,128)} %bitcast.104), kind=kCustom, calls=%fused_computation.1 | custom fusion | bytes 25166080 | tf_op jit(solution)/shard_map/scatter | solution.py:64
  38.4 5.8 %all-to-all-start.1 = ((f32[64,128,256]{2,1,0:T(8,128)}), f32[64,128,256]{2,1,0:T(8,128)}, u32[]{:S(2)}, u32[]{:S(2)}) async-start(f32[64,128,256]{2,1,0:T(8,128)} %scatter_fusion), calls=%async_computation.1 | async-start | bytes 16777216 | tf_op jit(solution)/shard_map/all_to_all | solution.py:71
  44.4 182.5 %all-to-all-done.1 = f32[64,128,256]{2,1,0:T(8,128)} async-done(((f32[64,128,256]{2,1,0:T(8,128)}), f32[64,128,256]{2,1,0:T(8,128)}, u32[]{:S(2)}, u32[]{:S(2)}) %all-to-all-start.1) | async-done | bytes 8388640 | tf_op jit(solution)/shard_map/all_to_all | solution.py:71
  226.9 2.5 broadcast_in_dim.11
  229.4 15.4 %scatter_fusion.1 = f32[32,128,256]{2,1,0:T(8,128)} fusion(f32[32,128,256]{2,1,0:T(8,128)} %broadcast_in_dim.11, s32[64]{0:T(128)S(1)} %fusion.37, f32[64,128,256]{2,1,0:T(8,128)} %all-to-all-done.1), kind=kCustom, calls=%fused_computation.2 | custom fusion | bytes 25166080 | tf_op jit(solution)/shard_map/scatter | solution.py:76
  244.8 10.9 %fusion = f32[256,256]{1,0:T(8,128)} fusion(f32[32,128,256]{2,1,0:T(8,128)} %scatter_fusion.1), kind=kOutput, calls=%fused_computation.9 | convolution fusion | flops 3221291008 | bytes 4456448 | tf_op jit(solution)/shard_map/dot_general | solution.py:18
  256.0 76.6 %all-gather.5.cloned.1.call-done = f32[8192,256]{1,0:T(8,128)} async-done(((f32[256,256]{1,0:T(8,128)}), f32[8192,256]{1,0:T(8,128)}) %all-gather.5.cloned.1.call-update) | async-done | bytes 8388624 | tf_op jit(solution)/shard_map/all_gather | solution.py:36
  332.6 3.9 reduce_sum.31
  336.7 11.7 %cholesky.130 = f32[128,128]{1,0:T(8,128)S(1)} custom-call(f32[128,128]{1,0:T(8,128)S(1)} %cholesky.194), custom_call_target="Cholesky" | custom-call | tf_op jit(solution)/shard_map/jit(cholesky)/cholesky | solution.py:10
  348.5 9.8 %custom-call.13 = f32[1,128,128]{1,2,0:T(8,128)S(1)} custom-call(f32[1,128,128]{2,1,0:T(8,128)S(1)} %get-tuple-element.55), custom_call_target="InvertDiagBlocksLowerTriangular" | custom-call | tf_op jit(solution)/shard_map/jit(cholesky)/cholesky | solution.py:10
  358.5 0.3 convolution_subtract_fusion.3
  358.8 11.7 %cholesky.147 = f32[128,128]{1,0:T(8,128)S(1)} custom-call(f32[128,128]{1,0:T(8,128)S(1)} %convolution_subtract_fusion.3), custom_call_target="Cholesky" | custom-call | tf_op jit(solution)/shard_map/jit(cholesky)/cholesky | solution.py:10
  370.5 0.7 compare_reduce_fusion.2
  372.6 4.0 while.4
  372.6 0.6 fusion.63
  373.2 1.4 bitcast_dynamic-update-slice_fusion.4
  374.6 0.6 fusion.63
  375.2 1.4 bitcast_dynamic-update-slice_fusion.4
  376.6 19.7 %custom-call.14 = f32[2,128,128]{1,2,0:T(8,128)S(1)} custom-call(f32[2,128,128]{2,1,0:T(8,128)S(1)} %get-tuple-element.18), custom_call_target="InvertDiagBlocksLowerTriangular" | custom-call | tf_op jit(solution)/shard_map/triangular_solve/custom-call.0 | solution.py:12
  396.3 0.3 fusion.23
  396.8 0.3 fusion.30
  397.2 5.5 fusion.1
  402.7 2.0 copy-done
  404.6 7.5 %convolution_multiply_fusion = f32[256,256]{1,0:T(8,128)} fusion(f32[4096,256]{1,0:T(8,128)S(1)} %fusion.1), kind=kOutput, calls=%fused_computation.7 | convolution fusion | flops 3221291008 | bytes 4456448 | tf_op jit(solution)/shard_map/dot_general | solution.py:18
  412.1 76.2 %all-gather.7.cloned.1.call-done = f32[8192,256]{1,0:T(8,128)} async-done(((f32[256,256]{1,0:T(8,128)}), f32[8192,256]{1,0:T(8,128)}) %all-gather.7.cloned.1.call-update) | async-done | bytes 8388624 | tf_op jit(solution)/shard_map/all_gather | solution.py:36
  488.3 3.9 reduce_sum.32
  492.4 11.7 %cholesky.164 = f32[128,128]{1,0:T(8,128)S(1)} custom-call(f32[128,128]{1,0:T(8,128)S(1)} %cholesky.197), custom_call_target="Cholesky" | custom-call | tf_op jit(solution)/shard_map/jit(cholesky)/cholesky | solution.py:10
  504.2 10.2 %custom-call.15 = f32[1,128,128]{1,2,0:T(8,128)S(1)} custom-call(f32[1,128,128]{2,1,0:T(8,128)S(1)} %get-tuple-element.51), custom_call_target="InvertDiagBlocksLowerTriangular" | custom-call | tf_op jit(solution)/shard_map/jit(cholesky)/cholesky | solution.py:10
  514.6 0.3 convolution_subtract_fusion.2
  514.9 11.7 %cholesky.181 = f32[128,128]{1,0:T(8,128)S(1)} custom-call(f32[128,128]{1,0:T(8,128)S(1)} %convolution_subtract_fusion.2), custom_call_target="Cholesky" | custom-call | tf_op jit(solution)/shard_map/jit(cholesky)/cholesky | solution.py:10
  526.6 0.6 compare_reduce_fusion
  527.3 0.6 compare_reduce_fusion.1
  529.2 1.2 fusion.15
  530.5 4.1 while.5
  530.5 0.6 fusion.64
  531.1 1.4 bitcast_dynamic-update-slice_fusion.5
  532.5 0.6 fusion.64
  533.1 1.4 bitcast_dynamic-update-slice_fusion.5
  534.6 19.8 %custom-call.16 = f32[2,128,128]{1,2,0:T(8,128)S(1)} custom-call(f32[2,128,128]{2,1,0:T(8,128)S(1)} %get-tuple-element.19), custom_call_target="InvertDiagBlocksLowerTriangular" | custom-call | tf_op jit(solution)/shard_map/triangular_solve/custom-call.0 | solution.py:12
  554.4 0.3 fusion.21
  555.0 0.3 fusion.26
  555.3 7.7 %fusion.5 = f32[4096,256]{1,0:T(8,128)} fusion(f32[4096,256]{1,0:T(8,128)} %copy-done, f32[128,256]{1,0:T(8,128)S(1)} %fusion.26, f32[128,256]{1,0:T(8,128)S(1)} %fusion.21), kind=kOutput, calls=%fused_computation.18 | convolution fusion | flops 3221291008 | bytes 8650752 | tf_op jit(solution)/shard_map/dot_general | solution.py:30
  (39 shorter events, 2.2 us)
Async XLA Ops:
  10.8 27.6 %all-to-all-start = ((f32[8,8,1]{1,2,0:T(1,128)}), f32[8,8,1]{1,2,0:T(1,128)S(1)}, u32[]{:S(2)}, u32[]{:S(2)}) async-start(f32[8,8,1]{1,2,0:T(1,128)} %bitcast.5), calls=%async_computation | async-start | bytes 8192 | tf_op jit(solution)/shard_map/all_to_all | solution.py:72
  38.4 188.5 %all-to-all-start.1 = ((f32[64,128,256]{2,1,0:T(8,128)}), f32[64,128,256]{2,1,0:T(8,128)}, u32[]{:S(2)}, u32[]{:S(2)}) async-start(f32[64,128,256]{2,1,0:T(8,128)} %scatter_fusion), calls=%async_computation.1 | async-start | bytes 16777216 | tf_op jit(solution)/shard_map/all_to_all | solution.py:71
  44.2 288.3 %all-gather.5.cloned.1.call-start = ((), (), s32[]{:S(2)}) async-start(), calls=%async_computation.2 | async-start | bytes 8650752 | tf_op jit(solution)/shard_map/all_gather | solution.py:36
  255.7 232.6 %all-gather.7.cloned.1.call-start = ((), (), s32[]{:S(2)}) async-start(), calls=%async_computation.3 | async-start | bytes 8650752 | tf_op jit(solution)/shard_map/all_gather | solution.py:36
  402.7 2.0 copy-start
Sparse Core Ops, SparseCore 0:
  255.9 76.6 all-gather.4
  412.3 76.0 all-gather.6
